TPU v7x, 256 devices: a whole 4x4x8 slice. The times are simulated.
256 devices in a mesh: dp: 8 (over y_hi, x), seq: 16 (over y_lo, z), segment: 2 (over core).
Axes of the slice: x: 4, y: 4 (y_hi: 2, y_lo: 2; y = y_hi * 2 + y_lo), z: 8, core: 2. Of those that a mesh axis runs over, the one named last changes fastest.
Arguments:
- saved_input: bfloat16 [2, 8, 8192, 256], P('segment', 'dp', 'seq'), may hold values from -6 to 6
- upstream: bfloat16 [8, 8192, 256], P('dp', 'seq'), may hold values from -6 to 6
- clip_lengths: int32 [8, 32], P('dp'), may hold values from 1 to 2048, 8192 in all within a row
- conv_a: bfloat16 [2, 3, 7, 256, 256], P('segment'), may hold values from -0.125 to 0.125
- bias_a: float32 [2, 3, 256], P('segment'), may hold values from -3 to 3
- conv_b: bfloat16 [2, 3, 256, 256], P('segment'), may hold values from -0.375 to 0.375
Outputs:
- section_input_grad: bfloat16 [2, 8, 8192, 256], P('segment', 'dp', 'seq')
- grad_conv_a: float32 [2, 3, 7, 256, 256], P('segment')
- grad_bias_a: float32 [2, 3, 256], P('segment')
- grad_conv_b: float32 [2, 3, 256, 256], P('segment')
Inputs may be any that keep to these rules, and one draw needn't show every extreme that they name: `clip_lengths`: each row's 32 lengths sum to 8192, and the longest is exactly 2048.
All inputs are finite; a program needn't handle non-finite values.
Results may differ from a plain program's by a relative error of at most 0.02.
Values may be sent and summed in bfloat16 or wider, within the bound.
No kernel may reach another device: no remote copies, remote signals or barrier semaphores. Data moves between devices by JAX's collectives and lax.ppermute only.
A program may use at most 128 MiB of HBM per device.

v0:
```python
import jax
import jax.numpy as jnp
from jax import lax
from jax.sharding import PartitionSpec as P

KERNEL = 7
UNITS = 3


def with_halo(cells, sides, width):
    for axis, dim in sides:
        count = lax.axis_size(axis)
        ends = count - 1
        head = lax.slice_in_dim(cells, 0, width, axis=dim)
        tail = lax.slice_in_dim(cells, cells.shape[dim] - width, cells.shape[dim], axis=dim)
        cells = jnp.concatenate(
            [
                lax.ppermute(tail, axis, [(i, (i + 1) % count) for i in range(ends)]),
                cells,
                lax.ppermute(head, axis, [((i + 1) % count, i) for i in range(ends)]),
            ],
            axis=dim,
        )
    return cells


def spread(value, axis, root):
    mine = lax.axis_index(axis) == root
    return lax.psum(jnp.where(mine, value, jnp.zeros_like(value)), axis)


def elu_act(value):
    return jnp.where(value > 0, value, jnp.expm1(jnp.minimum(value, 0.0)))


def elu_slope(value):
    return jnp.where(value > 0, 1.0, jnp.exp(jnp.minimum(value, 0.0)))


def spread_acts(active, reach):
    return with_halo(active, (("seq", 0),), reach)


def spread_grads(gate, reach):
    return with_halo(gate, (("seq", 0),), reach)


def shards(saved_input, upstream, clip_lengths, conv_a, bias_a, conv_b):
    stream = saved_input[0, 0]
    lengths = clip_lengths[0]
    weights_a = conv_a[0]
    biases_a = bias_a[0]
    weights_b = conv_b[0]
    frames = stream.shape[0]
    channels = stream.shape[1]
    inner = weights_a.shape[3]
    half = KERNEL // 2
    furthest = half * 3 ** (UNITS - 1)
    offset = lax.axis_index("seq") * frames
    is_decoder = lax.axis_index("segment") == 1
    clip_ends = jnp.cumsum(lengths)
    places = offset - furthest + jnp.arange(frames + 2 * furthest, dtype=jnp.int32)
    clip_of = jnp.sum((places[:, None] >= clip_ends[None, :]).astype(jnp.int32), axis=1)
    own_clip = clip_of[furthest : furthest + frames]

    def linked(shift_by):
        return (clip_of[furthest + shift_by : furthest + shift_by + frames] == own_clip)[:, None]

    stored = []
    for unit_idx in range(UNITS):
        dilation = 3**unit_idx
        reach = half * dilation
        active = elu_act(stream.astype(jnp.float32)).astype(jnp.bfloat16)
        padded = spread_acts(active, reach)
        tap_rows = jnp.concatenate(
            [
                jnp.where(
                    linked((tap_no - half) * dilation),
                    padded[
                        reach
                        + (tap_no - half) * dilation : reach
                        + (tap_no - half) * dilation
                        + frames
                    ],
                    jnp.zeros((), jnp.bfloat16),
                )
                for tap_no in range(KERNEL)
            ],
            axis=1,
        )
        pre_act = biases_a[unit_idx][None, :] + jnp.dot(
            tap_rows,
            weights_a[unit_idx].reshape(KERNEL * channels, inner),
            preferred_element_type=jnp.float32,
        )
        squashed = elu_act(pre_act).astype(jnp.bfloat16)
        next_stream = (
            stream.astype(jnp.float32)
            + jnp.dot(squashed, weights_b[unit_idx], preferred_element_type=jnp.float32)
        ).astype(jnp.bfloat16)
        stored.append((stream, tap_rows, pre_act, squashed))
        stream = next_stream

    def unit_back(unit_idx, grad_y):
        dilation = 3**unit_idx
        reach = half * dilation
        stream_in, tap_rows, pre_act, squashed = stored[unit_idx]
        grad_b = lax.dot_general(
            grad_y,
            weights_b[unit_idx],
            (((1,), (1,)), ((), ())),
            preferred_element_type=jnp.float32,
        )
        gate = (grad_b * elu_slope(pre_act)).astype(jnp.bfloat16)
        gate_padded = spread_grads(gate, reach)
        back_rows = jnp.concatenate(
            [
                jnp.where(
                    linked(-(tap_no - half) * dilation),
                    gate_padded[
                        reach
                        - (tap_no - half) * dilation : reach
                        - (tap_no - half) * dilation
                        + frames
                    ],
                    jnp.zeros((), jnp.bfloat16),
                )
                for tap_no in range(KERNEL)
            ],
            axis=1,
        )
        turned = jnp.transpose(weights_a[unit_idx], (0, 2, 1)).reshape(KERNEL * inner, channels)
        back = jnp.dot(back_rows, turned, preferred_element_type=jnp.float32)
        grad_next = (
            grad_y.astype(jnp.float32) + back * elu_slope(stream_in.astype(jnp.float32))
        ).astype(jnp.bfloat16)
        return (gate, grad_next)

    first_gates = [None] * UNITS
    first_grads = [None] * (UNITS + 1)
    grad_y = upstream[0]
    first_grads[UNITS] = grad_y
    for unit_idx in reversed(range(UNITS)):
        gate, grad_y = unit_back(unit_idx, grad_y)
        first_gates[unit_idx] = gate
        first_grads[unit_idx] = grad_y
    latent = lax.ppermute(grad_y, "segment", [(1, 0)])
    grads_a = [None] * UNITS
    grads_bias = [None] * UNITS
    grads_b = [None] * UNITS
    contract = (((0,), (0,)), ((), ()))
    grad_y = latent
    for unit_idx in reversed(range(UNITS)):
        stream_in, tap_rows, pre_act, squashed = stored[unit_idx]
        gate_two, grad_next = unit_back(unit_idx, grad_y)
        gate = jnp.where(is_decoder, first_gates[unit_idx], gate_two)
        grad_out = jnp.where(is_decoder, first_grads[unit_idx + 1], grad_y)
        unit_b = lax.dot_general(squashed, grad_out, contract, preferred_element_type=jnp.float32)
        unit_bias = jnp.sum(gate.astype(jnp.float32), axis=0)
        unit_a = lax.dot_general(
            tap_rows, gate, contract, preferred_element_type=jnp.float32
        ).reshape(KERNEL, channels, inner)
        grads_a[unit_idx] = unit_a
        grads_bias[unit_idx] = unit_bias
        grads_b[unit_idx] = unit_b
        grad_y = grad_next
    section_grad = jnp.where(is_decoder, first_grads[0], grad_y)
    rows_a = UNITS * KERNEL * channels
    rows_b = UNITS * inner
    packed = jnp.concatenate(
        [
            jnp.stack(grads_a).reshape(rows_a, inner),
            jnp.stack(grads_b).reshape(rows_b, channels),
            jnp.pad(jnp.stack(grads_bias), ((0, 8 - UNITS), (0, 0))),
        ],
        axis=0,
    )
    group = lax.axis_size("dp") * lax.axis_size("seq")
    rows = packed.shape[0]
    share = -(-rows // (group * 8)) * 8
    packed = jnp.pad(packed, ((0, share * group - rows), (0, 0)))
    packed = lax.psum_scatter(packed, ("dp", "seq"), scatter_dimension=0, tiled=True)
    packed = lax.all_gather(packed.astype(jnp.bfloat16), ("dp", "seq"), axis=0, tiled=True).astype(
        jnp.float32
    )
    total_a = packed[:rows_a].reshape(UNITS, KERNEL, channels, inner)
    total_b = packed[rows_a : rows_a + rows_b].reshape(UNITS, inner, channels)
    total_bias = packed[rows_a + rows_b : rows_a + rows_b + UNITS]
    return (section_grad[None, None], total_a[None], total_bias[None], total_b[None])


def solution(mesh):
    placed = (
        P("segment", "dp", "seq", None),
        P("dp", "seq", None),
        P("dp", None),
        P("segment", None, None, None, None),
        P("segment", None, None),
        P("segment", None, None, None),
    )
    return jax.shard_map(
        shards,
        mesh=mesh,
        in_specs=placed,
        out_specs=(
            P("segment", "dp", "seq", None),
            P("segment", None, None, None, None),
            P("segment", None, None),
            P("segment", None, None, None),
        ),
        check_vma=False,
    )
```

profile of v0, /device:TPU:0, one launch (start us, length us, event | category | flops | bytes accessed | tf_op | source)
XLA Modules:
  0.0 1517.2 jit_solution(5419906882155847757)
XLA Ops:
  7.2 1.2 fusion.28
  8.4 1.3 collective-permute-start.1
  9.7 4.5 collective-permute-start
  15.6 3.7 slice_bitcast_fusion.2
  21.9 2.1 collective-permute-start.2
  24.1 1.3 collective-permute-start.3
  25.9 3.7 collective-permute-done.3
  31.7 4.9 collective-permute-start.4
  36.7 1.3 collective-permute-start.5
  38.6 3.7 collective-permute-done.5
  44.9 1.3 collective-permute-start.6
  46.2 2.2 copy.20
  48.4 5.8 collective-permute-start.7
  54.3 0.8 fusion.124
  55.1 0.8 fusion.121
  55.9 0.8 fusion.161
  58.3 1.3 fusion.13
  59.6 1.3 collective-permute-start.8
  60.9 2.2 copy.21
  63.2 4.7 collective-permute-start.9
  68.3 0.8 collective-permute-done.9
  70.7 1.3 fusion.14
  72.6 1.3 collective-permute-start.10
  73.9 1.4 copy.22
  75.3 5.1 collective-permute-start.11
  80.4 0.8 fusion.52
  81.3 0.8 fusion.49
  82.1 0.8 fusion.153
  84.1 1.3 collective-permute-start.12
  85.4 2.1 collective-permute-done.12
  87.6 1.5 convert_reduce_fusion
  89.1 2.3 fusion.199
  91.4 4.1 collective-permute-start.14
  95.5 1.3 collective-permute-start.13
  97.3 5.1 collective-permute-done.13
  105.8 1.3 collective-permute-start.15
  107.6 6.2 collective-permute-start.16
  114.2 0.9 collective-permute-done.16
  118.7 3.3 select_maximum_fusion
  122.1 728.6 %reduce-scatter.2.cloned.1.call-done = f32[56,256]{1,0:T(8,128)} async-done(((f32[7168,256]{1,0:T(8,128)}), f32[56,256]{1,0:T(8,128)}) %reduce-scatter.2.cloned.1.call-update) | async-done | bytes 57360 | tf_op jit(solution)/shard_map/reduce_scatter | solution.py:182
  850.7 1.4 convert_element_type.154
  852.1 1.3 collective-permute-start.17
  853.5 4.7 collective-permute-start.18
  858.6 0.8 collective-permute-done.18
  859.9 1.4 fusion.19
  861.3 641.2 %all-gather.2.cloned.1.call-done = bf16[7168,256]{1,0:T(8,128)(2,1)} async-done(((bf16[56,256]{1,0:T(8,128)(2,1)}), bf16[7168,256]{1,0:T(8,128)(2,1)}) %all-gather.2.cloned.1.call-update) | async-done | bytes 3670032 | tf_op jit(solution)/shard_map/all_gather | solution.py:183
  1503.7 1.9 slice.611
  1505.7 4.7 slice.609
  (263 shorter events, 24.8 us)
Async XLA Ops:
  7.2 843.5 %reduce-scatter.2.cloned.1.call-start = ((), (), s32[]{:S(2)}) async-start(), calls=%async_computation.1 | async-start | bytes 7397376 | tf_op jit(solution)/shard_map/reduce_scatter | solution.py:182
  8.4 11.6 collective-permute-start.1
  9.7 9.6 collective-permute-start
  15.4 10.4 copy-start.28
  15.4 22.7 %copy-start.51 = (pred[512]{0:T(512)(128)(4,1)}, pred[512]{0:T(512)(128)(4,1)S(1)}, u32[]{:S(2)}) copy-start(pred[512]{0:T(512)(128)(4,1)S(1)} %get-tuple-element.41) | copy-start | bytes 1540
  15.4 27.1 %copy-start.54 = (pred[512]{0:T(512)(128)(4,1)}, pred[512]{0:T(512)(128)(4,1)S(1)}, u32[]{:S(2)}) copy-start(pred[512]{0:T(512)(128)(4,1)S(1)} %get-tuple-element.37) | copy-start | bytes 1540
  15.5 10.1 copy-start.34
  15.5 14.1 copy-start.21
  15.5 14.2 copy-start.37
  15.5 22.7 %copy-start.40 = (pred[512]{0:T(512)(128)(4,1)}, pred[512]{0:T(512)(128)(4,1)S(1)}, u32[]{:S(2)}) copy-start(pred[512]{0:T(512)(128)(4,1)S(1)} %get-tuple-element.29) | copy-start | bytes 1540
  15.5 22.9 %copy-start.23 = (pred[512]{0:T(512)(128)(4,1)}, pred[512]{0:T(512)(128)(4,1)S(1)}, u32[]{:S(2)}) copy-start(pred[512]{0:T(512)(128)(4,1)S(1)} %get-tuple-element.33) | copy-start | bytes 1540
  15.6 26.8 %copy-start.26 = (pred[512]{0:T(512)(128)(4,1)}, pred[512]{0:T(512)(128)(4,1)S(1)}, u32[]{:S(2)}) copy-start(pred[512]{0:T(512)(128)(4,1)S(1)} %get-tuple-element.30) | copy-start | bytes 1540
  15.6 27.1 %copy-start.43 = (pred[512]{0:T(512)(128)(4,1)}, pred[512]{0:T(512)(128)(4,1)S(1)}, u32[]{:S(2)}) copy-start(pred[512]{0:T(512)(128)(4,1)S(1)} %get-tuple-element.28) | copy-start | bytes 1540
  21.9 9.4 copy-start.11
  21.9 3.5 collective-permute-start.2
  24.1 5.5 collective-permute-start.3
  31.7 25.5 %copy-start.17 = (f32[512,256]{1,0:T(8,128)}, f32[512,256]{1,0:T(8,128)S(1)}, u32[]{:S(2)}) copy-start(f32[512,256]{1,0:T(8,128)S(1)} %get-tuple-element.48) | copy-start | bytes 1572868
  31.7 6.4 collective-permute-start.4
  36.7 5.6 collective-permute-start.5
  44.9 9.3 collective-permute-start.6
  48.4 8.5 copy-start.41
  48.4 8.6 copy-start.52
  48.4 8.8 copy-start.9
  48.4 8.8 copy-start.58
  48.4 8.3 collective-permute-start.7
  58.3 9.6 copy-start.27
  58.3 9.7 copy-start.38
  58.3 9.9 copy-start.22
  59.6 8.3 collective-permute-start.8
  63.2 6.0 collective-permute-start.9
  72.6 7.9 collective-permute-start.10
  75.3 7.7 collective-permute-start.11
  84.1 3.4 collective-permute-start.12
  87.6 9.2 copy-start.62
  89.1 13.3 copy-start.44
  91.4 11.1 copy-start.55
  91.4 11.4 collective-permute-start.14
  95.5 6.8 collective-permute-start.13
  105.8 9.4 copy-start.36
  105.8 7.9 collective-permute-start.15
  107.6 7.5 collective-permute-start.16
  122.0 736.3 %copy-start.33 = (pred[512]{0:T(512)(128)(4,1)S(1)}, pred[512]{0:T(512)(128)(4,1)}, u32[]{:S(2)}) copy-start(pred[512]{0:T(512)(128)(4,1)} %copy-done.32) | copy-start | bytes 1540
  122.0 736.4 %copy-start.31 = (pred[512]{0:T(512)(128)(4,1)S(1)}, pred[512]{0:T(512)(128)(4,1)}, u32[]{:S(2)}) copy-start(pred[512]{0:T(512)(128)(4,1)} %copy-done.30) | copy-start | bytes 1540
  122.0 737.4 %copy-start.50 = (pred[512]{0:T(512)(128)(4,1)S(1)}, pred[512]{0:T(512)(128)(4,1)}, u32[]{:S(2)}) copy-start(pred[512]{0:T(512)(128)(4,1)} %copy-done.48) | copy-start | bytes 1540
  122.0 737.5 %copy-start.47 = (pred[512]{0:T(512)(128)(4,1)S(1)}, pred[512]{0:T(512)(128)(4,1)}, u32[]{:S(2)}) copy-start(pred[512]{0:T(512)(128)(4,1)} %copy-done.45) | copy-start | bytes 1540
  122.0 1380.4 %all-gather.2.cloned.1.call-start = ((), (), s32[]{:S(2)}) async-start(), calls=%async_computation.2 | async-start | bytes 3698688 | tf_op jit(solution)/shard_map/all_gather | solution.py:183
  852.1 6.0 collective-permute-start.17
  853.5 6.0 collective-permute-start.18
  (48 other events, 238.9 us)
Sparse Core Ops, SparseCore 0:
  122.1 728.4 reduce-scatter.1
  853.0 649.4 all-gather.1
where the time goes:
time: 1520 us
  waiting for transfers between devices  1390 us (91%)
  starting transfers between devices  55.1 us (4%)
  local copies, waits for them, and re-layouts  23.3 us (2%)
  other arithmetic  18.5 us (1%)
  matrix products  17.3 us (1%)
  between operations  15.9 us (1%)
    reduce_scatter x1, waiting for transfers between devices, shards(): lax.psum_scatter(packed, ('dp', 'seq'), scatter_dimension=0, tiled=True)  729 us
    all_gather x1, waiting for transfers between devices, shards(): lax.all_gather(packed.astype(jnp.bfloat16), ('dp', 'seq'), axis=0, tiled=...  641 us
    ppermute x9, starting transfers between devices, with_halo(): lax.ppermute(tail, axis, [(i, (i + 1) % count) for i in range(ends)])  42.1 us
  transfers between devices with their start and end apart: 21, of which 10 were waited for; matrix products, arithmetic and copies ran while one was open for 1% of the time, Pallas kernels for 0%

commit v1 on v0

--- a/solution.py
+++ b/solution.py
@@ -5,6 +5,12 @@
 
 KERNEL = 7
 UNITS = 3
+
+
+def mix_tails(local_x, a_name):
+    n_now = lax.all_to_all(jnp.stack(lax.axis_size(a_name) * [local_x], 0), a_name, 0, 0)
+    outcome_arr = jnp.concatenate(n_now, 0)
+    return outcome_arr
 
 
 def with_halo(cells, sides, width):
@@ -180,9 +186,7 @@
     share = -(-rows // (group * 8)) * 8
     packed = jnp.pad(packed, ((0, share * group - rows), (0, 0)))
     packed = lax.psum_scatter(packed, ("dp", "seq"), scatter_dimension=0, tiled=True)
-    packed = lax.all_gather(packed.astype(jnp.bfloat16), ("dp", "seq"), axis=0, tiled=True).astype(
-        jnp.float32
-    )
+    packed = mix_tails(packed.astype(jnp.bfloat16), ("dp", "seq")).astype(jnp.float32)
     total_a = packed[:rows_a].reshape(UNITS, KERNEL, channels, inner)
     total_b = packed[rows_a : rows_a + rows_b].reshape(UNITS, inner, channels)
     total_bias = packed[rows_a + rows_b : rows_a + rows_b + UNITS]

time: 1520 us -> 929 us (0.61)
  waiting for transfers between devices: 1390 us -> 787 us
    all_gather x1 -> x0, waiting for transfers between devices: 641 us -> none  [shards(): lax.all_gather(packed.astype(jnp.bfloat16), ('dp', 'seq'), axis=0, tiled=...]
    ppermute x9, waiting for transfers between devices: 12.5 us -> 43.4 us  [with_halo(): lax.ppermute(head, axis, [((i + 1) % count, i) for i in range(ends)])]
  transfers between devices with their start and end apart: 21 -> 21, of which waited for: 10 -> 10; matrix products, arithmetic and copies ran while one was open for 1% -> 2% of each run, Pallas kernels for 0% -> 0%
where the time goes in v1:
time: 929 us; the launch traced here: 927 us
  waiting for transfers between devices  787 us (85%)
  starting transfers between devices  62.9 us (7%)
  local copies, waits for them, and re-layouts  23.7 us (3%)
  other arithmetic  20.5 us (2%)
  matrix products  17.3 us (2%)
  between operations  15.9 us (2%)
    reduce_scatter x1, waiting for transfers between devices, shards(): lax.psum_scatter(packed, ('dp', 'seq'), scatter_dimension=0, tiled=True)  733 us
    ppermute x9, waiting for transfers between devices, with_halo(): lax.ppermute(head, axis, [((i + 1) % count, i) for i in range(ends)])  43.4 us
    ppermute x9, starting transfers between devices, with_halo(): lax.ppermute(tail, axis, [(i, (i + 1) % count) for i in range(ends)])  42.5 us
  transfers between devices with their start and end apart: 21, of which 10 were waited for; matrix products, arithmetic and copies ran while one was open for 2% of the time, Pallas kernels for 0%

profile of v1, /device:TPU:0, one launch (start us, length us, event | category | flops | bytes accessed | tf_op | source)
XLA Modules:
  0.0 927.2 jit_solution(17136986715719548265)
XLA Ops:
  7.2 1.2 fusion.28
  8.4 2.1 collective-permute-start
  10.5 1.3 collective-permute-start.1
  13.2 3.7 slice_bitcast_fusion.2
  19.5 4.5 collective-permute-start.2
  24.1 1.3 collective-permute-start.3
  25.9 3.7 collective-permute-done.3
  31.7 4.8 collective-permute-start.4
  36.6 1.3 collective-permute-start.5
  38.5 4.9 collective-permute-done.5
  46.0 1.3 collective-permute-start.6
  47.3 2.2 copy.20
  49.6 5.9 collective-permute-start.7
  55.5 0.8 fusion.124
  59.5 1.3 fusion.13
  60.8 1.3 collective-permute-start.8
  62.1 2.2 copy.21
  64.4 4.7 collective-permute-start.9
  69.6 0.8 collective-permute-done.9
  71.9 1.3 fusion.14
  73.8 1.3 collective-permute-start.10
  75.1 1.4 copy.22
  76.6 5.1 collective-permute-start.11
  81.7 0.8 fusion.52
  82.5 0.8 fusion.49
  83.4 0.8 fusion.153
  85.4 1.3 collective-permute-start.12
  86.7 2.1 collective-permute-done.12
  88.8 1.5 convert_reduce_fusion
  90.4 2.3 fusion.199
  92.7 1.3 collective-permute-start.13
  94.0 4.7 collective-permute-start.14
  103.1 1.3 collective-permute-start.15
  104.9 5.9 collective-permute-start.16
  111.3 0.9 collective-permute-done.16
  115.7 3.2 select_maximum_fusion
  119.0 732.7 %reduce-scatter.2.cloned.1.call-done = f32[56,256]{1,0:T(8,128)} async-done(((f32[7168,256]{1,0:T(8,128)}), f32[56,256]{1,0:T(8,128)}) %reduce-scatter.2.cloned.1.call-update) | async-done | bytes 57360 | tf_op jit(solution)/shard_map/reduce_scatter | solution.py:188
  851.7 0.8 convert_element_type.157
  852.5 2.1 stack.29
  854.6 7.4 all-to-all-start
  862.1 1.3 collective-permute-start.17
  863.4 4.7 collective-permute-start.18
  868.1 34.7 %collective-permute-done.17 = bf16[3,256]{1,0:T(4,128)(2,1)S(1)} collective-permute-done((bf16[3,256]{1,0:T(4,128)(2,1)S(1)}, bf16[3,256]{1,0:T(4,128)(2,1)S(1)}, u32[]{:S(2)}, u32[]{:S(2)}) %collective-permute-start.17) | collective-permute-done | bytes 1568 | tf_op jit(solution)/shard_map/ppermute | solution.py:26
  903.8 1.4 fusion.19
  905.2 6.3 all-to-all-done
  911.6 2.6 convert_element_type.158
  914.2 0.9 slice.612
  915.7 4.7 slice.610
  (268 shorter events, 26.1 us)
Async XLA Ops:
  7.2 844.6 %reduce-scatter.2.cloned.1.call-start = ((), (), s32[]{:S(2)}) async-start(), calls=%async_computation.2 | async-start | bytes 7397376 | tf_op jit(solution)/shard_map/reduce_scatter | solution.py:188
  8.4 8.5 collective-permute-start
  10.5 7.0 collective-permute-start.1
  12.9 12.8 %copy-start.28 = (pred[512]{0:T(512)(128)(4,1)}, pred[512]{0:T(512)(128)(4,1)S(1)}, u32[]{:S(2)}) copy-start(pred[512]{0:T(512)(128)(4,1)S(1)} %get-tuple-element.40) | copy-start | bytes 1540
  12.9 25.1 %copy-start.51 = (pred[512]{0:T(512)(128)(4,1)}, pred[512]{0:T(512)(128)(4,1)S(1)}, u32[]{:S(2)}) copy-start(pred[512]{0:T(512)(128)(4,1)S(1)} %get-tuple-element.41) | copy-start | bytes 1540
  13.0 30.6 %copy-start.54 = (pred[512]{0:T(512)(128)(4,1)}, pred[512]{0:T(512)(128)(4,1)S(1)}, u32[]{:S(2)}) copy-start(pred[512]{0:T(512)(128)(4,1)S(1)} %get-tuple-element.37) | copy-start | bytes 1540
  13.1 12.5 %copy-start.34 = (pred[512]{0:T(512)(128)(4,1)}, pred[512]{0:T(512)(128)(4,1)S(1)}, u32[]{:S(2)}) copy-start(pred[512]{0:T(512)(128)(4,1)S(1)} %get-tuple-element.32) | copy-start | bytes 1540
  13.1 16.5 %copy-start.21 = (pred[512]{0:T(512)(128)(4,1)}, pred[512]{0:T(512)(128)(4,1)S(1)}, u32[]{:S(2)}) copy-start(pred[512]{0:T(512)(128)(4,1)S(1)} %get-tuple-element.34) | copy-start | bytes 1540
  13.1 16.7 %copy-start.37 = (pred[512]{0:T(512)(128)(4,1)}, pred[512]{0:T(512)(128)(4,1)S(1)}, u32[]{:S(2)}) copy-start(pred[512]{0:T(512)(128)(4,1)S(1)} %get-tuple-element.31) | copy-start | bytes 1540
  13.1 25.1 %copy-start.40 = (pred[512]{0:T(512)(128)(4,1)}, pred[512]{0:T(512)(128)(4,1)S(1)}, u32[]{:S(2)}) copy-start(pred[512]{0:T(512)(128)(4,1)S(1)} %get-tuple-element.29) | copy-start | bytes 1540
  13.1 25.2 %copy-start.23 = (pred[512]{0:T(512)(128)(4,1)}, pred[512]{0:T(512)(128)(4,1)S(1)}, u32[]{:S(2)}) copy-start(pred[512]{0:T(512)(128)(4,1)S(1)} %get-tuple-element.33) | copy-start | bytes 1540
  13.1 30.3 %copy-start.26 = (pred[512]{0:T(512)(128)(4,1)}, pred[512]{0:T(512)(128)(4,1)S(1)}, u32[]{:S(2)}) copy-start(pred[512]{0:T(512)(128)(4,1)S(1)} %get-tuple-element.30) | copy-start | bytes 1540
  13.1 30.6 %copy-start.43 = (pred[512]{0:T(512)(128)(4,1)}, pred[512]{0:T(512)(128)(4,1)S(1)}, u32[]{:S(2)}) copy-start(pred[512]{0:T(512)(128)(4,1)S(1)} %get-tuple-element.28) | copy-start | bytes 1540
  19.5 11.8 %copy-start.11 = (f32[512,256]{1,0:T(8,128)}, f32[512,256]{1,0:T(8,128)S(1)}, u32[]{:S(2)}) copy-start(f32[512,256]{1,0:T(8,128)S(1)} %get-tuple-element.46) | copy-start | bytes 1572868
  19.5 5.9 collective-permute-start.2
  24.1 5.5 collective-permute-start.3
  31.7 26.7 %copy-start.17 = (f32[512,256]{1,0:T(8,128)}, f32[512,256]{1,0:T(8,128)S(1)}, u32[]{:S(2)}) copy-start(f32[512,256]{1,0:T(8,128)S(1)} %get-tuple-element.48) | copy-start | bytes 1572868
  31.7 6.3 collective-permute-start.4
  36.6 6.8 collective-permute-start.5
  46.0 9.4 %collective-permute-start.6 = (bf16[27,256]{1,0:T(8,128)(2,1)}, bf16[27,256]{1,0:T(8,128)(2,1)S(1)}, u32[]{:S(2)}, u32[]{:S(2)}) collective-permute-start(bf16[27,256]{1,0:T(8,128)(2,1)} %get-tuple-element.21), channel_id=1, source_target_pairs={{2,0},{4,2},{6,4},{8,6},{10,8},{12,10},{14,12},{16,14},{18,16},{20... | collective-permute-start | bytes 41480 | tf_op jit(solution)/shard_map/ppermute | solution.py:26
  49.6 8.9 copy-start.9
  49.6 8.9 copy-start.58
  49.6 8.4 collective-permute-start.7
  59.5 9.6 %copy-start.27 = (pred[512]{0:T(512)(128)(4,1)S(1)}, pred[512]{0:T(512)(128)(4,1)}, u32[]{:S(2)}) copy-start(pred[512]{0:T(512)(128)(4,1)} %copy-done.26) | copy-start | bytes 1540
  59.5 9.8 %copy-start.38 = (pred[512]{0:T(512)(128)(4,1)S(1)}, pred[512]{0:T(512)(128)(4,1)}, u32[]{:S(2)}) copy-start(pred[512]{0:T(512)(128)(4,1)} %copy-done.37) | copy-start | bytes 1540
  59.5 9.9 %copy-start.22 = (pred[512]{0:T(512)(128)(4,1)S(1)}, pred[512]{0:T(512)(128)(4,1)}, u32[]{:S(2)}) copy-start(pred[512]{0:T(512)(128)(4,1)} %copy-done.21) | copy-start | bytes 1540
  60.8 8.3 collective-permute-start.8
  64.4 6.0 collective-permute-start.9
  73.8 7.9 collective-permute-start.10
  76.6 7.7 collective-permute-start.11
  85.4 3.4 collective-permute-start.12
  88.8 9.9 %copy-start.62 = (bf16[512,256]{1,0:T(8,128)(2,1)}, bf16[512,256]{1,0:T(8,128)(2,1)S(1)}, u32[]{:S(2)}) copy-start(bf16[512,256]{1,0:T(8,128)(2,1)S(1)} %collective-permute-done.12) | copy-start | bytes 786436
  90.4 8.8 copy-start.44
  92.7 6.5 collective-permute-start.13
  94.0 6.1 collective-permute-start.14
  103.1 9.2 copy-start.36
  103.1 7.7 collective-permute-start.15
  104.9 7.3 collective-permute-start.16
  854.6 48.4 %copy-start.33 = (pred[512]{0:T(512)(128)(4,1)S(1)}, pred[512]{0:T(512)(128)(4,1)}, u32[]{:S(2)}) copy-start(pred[512]{0:T(512)(128)(4,1)} %copy-done.32) | copy-start | bytes 1540
  854.6 48.5 %copy-start.31 = (pred[512]{0:T(512)(128)(4,1)S(1)}, pred[512]{0:T(512)(128)(4,1)}, u32[]{:S(2)}) copy-start(pred[512]{0:T(512)(128)(4,1)} %copy-done.30) | copy-start | bytes 1540
  854.6 57.0 %all-to-all-start = ((bf16[128,56,256]{2,1,0:T(8,128)(2,1)}), bf16[128,56,256]{2,1,0:T(8,128)(2,1)}, u32[]{:S(2)}, u32[]{:S(2)}) async-start(bf16[128,56,256]{2,1,0:T(8,128)(2,1)} %stack.29), calls=%async_computation.1 | async-start | bytes 7340032 | tf_op jit(solution)/shard_map/all_to_all | solution.py:11
  862.1 41.3 %copy-start.50 = (pred[512]{0:T(512)(128)(4,1)S(1)}, pred[512]{0:T(512)(128)(4,1)}, u32[]{:S(2)}) copy-start(pred[512]{0:T(512)(128)(4,1)} %copy-done.48) | copy-start | bytes 1540
  862.1 41.4 %copy-start.47 = (pred[512]{0:T(512)(128)(4,1)S(1)}, pred[512]{0:T(512)(128)(4,1)}, u32[]{:S(2)}) copy-start(pred[512]{0:T(512)(128)(4,1)} %copy-done.45) | copy-start | bytes 1540
  862.1 40.7 %collective-permute-start.17 = (bf16[3,256]{1,0:T(4,128)(2,1)S(1)}, bf16[3,256]{1,0:T(4,128)(2,1)S(1)}, u32[]{:S(2)}, u32[]{:S(2)}) collective-permute-start(bf16[3,256]{1,0:T(4,128)(2,1)S(1)} %get-tuple-element.11), channel_id=1, source_target_pairs={{2,0},{4,2},{6,4},{8,6},{10,8},{12,10},{14,12},{16,14},{18,16},{20... | collective-permute-start | bytes 4616 | tf_op jit(solution)/shard_map/ppermute | solution.py:26
  863.4 40.4 %copy-start.6 = (bf16[7,256,256]{2,1,0:T(8,128)(2,1)S(1)}, bf16[7,256,256]{2,1,0:T(8,128)(2,1)}, u32[]{:S(2)}) copy-start(bf16[7,256,256]{2,1,0:T(8,128)(2,1)} %copy.22) | copy-start | bytes 2752516
  863.4 40.4 %copy-start.61 = (bf16[512,256]{1,0:T(8,128)(2,1)S(1)}, bf16[512,256]{1,0:T(8,128)(2,1)}, u32[]{:S(2)}) copy-start(bf16[512,256]{1,0:T(8,128)(2,1)} %copy-done.60) | copy-start | bytes 786436
  863.4 40.4 %copy-start.76 = (bf16[512,256]{1,0:T(8,128)(2,1)S(1)}, bf16[512,256]{1,0:T(8,128)(2,1)}, u32[]{:S(2)}) copy-start(bf16[512,256]{1,0:T(8,128)(2,1)} %copy-done.75) | copy-start | bytes 786436
  863.4 39.9 %collective-permute-start.18 = (bf16[3,256]{1,0:T(4,128)(2,1)S(1)}, bf16[3,256]{1,0:T(4,128)(2,1)S(1)}, u32[]{:S(2)}, u32[]{:S(2)}) collective-permute-start(bf16[3,256]{1,0:T(4,128)(2,1)S(1)} %get-tuple-element.10), channel_id=1, source_target_pairs={{0,2},{2,4},{4,6},{6,8},{8,10},{10,12},{12,14},{14,16},{16,18},{18... | collective-permute-start | bytes 4616 | tf_op jit(solution)/shard_map/ppermute | solution.py:24
  (50 other events, 234.9 us)
Sparse Core Ops, SparseCore 0:
  119.1 732.5 reduce-scatter.1
